TPU v7x, 256 devices: a whole 4x4x8 slice. The times are simulated.
256 devices in a mesh: depth: 16 (over y_hi, z), filt: 16 (over x, y_lo, core).
Axes of the slice: x: 4, y: 4 (y_hi: 2, y_lo: 2; y = y_hi * 2 + y_lo), z: 8, core: 2. Of those that a mesh axis runs over, the one named last changes fastest.
Arguments:
- features: bfloat16 [32, 128, 4096], P('depth', 'filt'), may hold values from -6 to 6
- first_kernel: bfloat16 [3, 3, 3, 256, 128], P(None, None, None, 'filt'), may hold values from -0.109375 to 0.109375
- first_bias: float32 [256], P('filt'), may hold values from -1.5 to 1.5
- second_kernel: bfloat16 [3, 3, 3, 256, 256], P(None, None, None, 'filt'), may hold values from -0.078125 to 0.078125
- second_bias: float32 [256], P('filt'), may hold values from -1.5 to 1.5
Outputs:
- activated: bfloat16 [32, 256, 4096], P('depth', 'filt')
All inputs are finite; a program needn't handle non-finite values.
Results may differ from a plain program's by a relative error of at most 0.0047.
Values may be sent and summed in bfloat16 or wider, within the bound.
No kernel may reach another device: no remote copies, remote signals or barrier semaphores. Data moves between devices by JAX's collectives and lax.ppermute only.
A program may use at most 64 MiB of HBM per device.

v0:
```python
import jax
import jax.numpy as jnp
from jax import lax
from jax.sharding import PartitionSpec as P

SIDE = 64


leak_slope = 0.3


def tap_products(block, kernel):
    outs, chans = kernel.shape[3], kernel.shape[4]
    taps = kernel.reshape(27 * outs, chans)
    products = jnp.einsum("tc,pcq->tpq", taps, block, preferred_element_type=jnp.float32)
    return products.reshape(3, 3, 3, outs, block.shape[0], block.shape[2])


def spatial_sum(part):
    cells = part.shape[-1]
    column = jnp.arange(cells, dtype=jnp.int32) % SIDE
    reach = SIDE + 1
    framed = jnp.pad(part, ((0, 0), (0, 0), (0, 0), (reach, reach)))
    total = None
    for tap_h in range(3):
        for tap_w in range(3):
            begin = reach + (tap_h - 1) * SIDE + (tap_w - 1)
            window = framed[tap_h, tap_w, :, begin : begin + cells]
            moved = column + (tap_w - 1)
            usable = (moved >= 0) & (moved < SIDE)
            window = jnp.where(usable[None, :], window, jnp.zeros_like(window))
            total = window if total is None else total + window
    return total


def conv_sum(block, kernel):
    planes = block.shape[0]
    products = tap_products(block, kernel)
    count = lax.axis_size("depth")
    forward = [(i, i + 1) for i in range(count - 1)]
    backward = [(i + 1, i) for i in range(count - 1)]
    to_above = spatial_sum(products[0, :, :, :, planes - 1])
    to_below = spatial_sum(products[2, :, :, :, 0])
    from_below = lax.ppermute(to_above, "depth", forward)
    from_above = lax.ppermute(to_below, "depth", backward)
    rows = []
    for plane in range(planes):
        total = None
        for tap_d in range(3):
            source = plane + tap_d - 1
            if 0 <= source < planes:
                piece = spatial_sum(products[tap_d, :, :, :, source])
                total = piece if total is None else total + piece
        if plane == 0:
            total = total + from_below
        if plane == planes - 1:
            total = total + from_above
        rows.append(total)
    return jnp.stack(rows)


def activate(summed, bias):
    shifted = summed + bias[None, :, None]
    return jnp.where(shifted > 0, shifted, leak_slope * shifted).astype(jnp.bfloat16)


def local(features, first_kernel, first_bias, second_kernel, second_bias):
    whole_in = lax.all_gather(features, "filt", axis=1, tiled=True)
    hidden = activate(conv_sum(whole_in, first_kernel), first_bias)
    whole_mid = lax.all_gather(hidden, "filt", axis=1, tiled=True)
    return activate(conv_sum(whole_mid, second_kernel), second_bias)


def solution(mesh):
    in_specs = (
        P("depth", "filt", None),
        P(None, None, None, "filt", None),
        P("filt"),
        P(None, None, None, "filt", None),
        P("filt"),
    )
    out_specs = P("depth", "filt", None)
    return jax.shard_map(local, mesh=mesh, in_specs=in_specs, out_specs=out_specs, check_vma=False)
```

profile of v0, /device:TPU:17, one launch (start us, length us, event | category | flops | bytes accessed | tf_op | source)
XLA Modules:
  0.0 185.2 jit_solution(15106968585745396712)
XLA Ops:
  6.5 0.0 copy-start
  6.5 0.0 all-gather.3.cloned.1.call-start
  6.5 0.7 all-gather.3.cloned.1.call-update
  7.3 0.0 all-gather.5.cloned.1.call-start
  7.3 41.2 %all-gather.3.cloned.1.call-done = bf16[2,128,4096]{2,1,0:T(8,128)(2,1)} async-done(((bf16[2,8,4096]{2,1,0:T(8,128)(2,1)}), bf16[2,128,4096]{2,1,0:T(8,128)(2,1)}) %all-gather.3.cloned.1.call-update) | async-done | bytes 2097168 | tf_op jit(solution)/shard_map/all_gather | solution.py:68
  48.5 8.7 %fusion = f32[3,3,3,16,2,4096]{5,3,4,2,1,0:T(8,128)} fusion(bf16[2,128,4096]{2,1,0:T(8,128)(2,1)} %all-gather.3.cloned.1.call-done, bf16[3,3,3,16,128]{4,3,2,1,0:T(8,128)(2,1)} %param.6), kind=kOutput, calls=%fused_computation.12 | convolution fusion | flops 905969664 | bytes 16363520 | tf_op jit(solution)/shard_map/tc,pcq->tpq/dot_general | solution.py:15
  57.2 9.7 %slice_bitcast_fusion.11 = (f32[3,3,16,4096]{3,2,1,0:T(8,128)}, f32[3,3,16,4096]{3,2,1,0:T(8,128)}, f32[3,3,16,4096]{3,2,1,0:T(8,128)S(1)}, f32[3,3,16,4096]{3,2...) fusion(f32[3,3,3,16,2,4096]{5,3,4,2,1,0:T(8,128)} %fusion), kind=kLoop, calls=%fused_computation.11 | loop fusion | bytes 28311552 | tf_op jit(solution)/shard_map/squeeze | solution.py:52
  66.9 0.0 copy-start.4
  66.9 0.0 copy-start.5
  66.9 2.9 %fusion.63 = (f32[16,4096]{1,0:T(8,128)S(1)}, f32[16,4096]{1,0:T(8,128)S(1)}) fusion(f32[3,3,16,4096]{3,2,1,0:T(8,128)S(1)} %get-tuple-element.13, pred[4096]{0:T(1024)(128)(4,1)S(1)} %get-tuple-element.23, pred[4096]{0:T(1024)(128)(4,1)S(1)} %fusion.329, pred[4096]{0:T(1024)(128)(4,1)S(1)} %get-tuple-element.24, f32[3,3,16,4096]{3,2,1,0:T(8,128)} %get-tuple-element.15), kind=kLoop, calls=%fused_computation.175 | loop fusion | flops 2228224 | bytes 5779456 | tf_op jit(solution)/shard_map/add | solution.py:32
  69.8 3.2 %collective-permute-start = (f32[16,4096]{1,0:T(8,128)S(1)}, f32[16,4096]{1,0:T(8,128)S(1)}, u32[]{:S(2)}, u32[]{:S(2)}) collective-permute-start(f32[16,4096]{1,0:T(8,128)S(1)} %get-tuple-element.21), channel_id=1, source_target_pairs={{0,16},{16,32},{32,48},{48,64},{64,80},{80,96},{96,112},{112,128},... | collective-permute-start | bytes 786440 | tf_op jit(solution)/shard_map/ppermute | solution.py:44
  73.0 5.7 %collective-permute-start.1 = (f32[16,4096]{1,0:T(8,128)S(1)}, f32[16,4096]{1,0:T(8,128)S(1)}, u32[]{:S(2)}, u32[]{:S(2)}) collective-permute-start(f32[16,4096]{1,0:T(8,128)S(1)} %get-tuple-element.22), channel_id=1, source_target_pairs={{16,0},{32,16},{48,32},{64,48},{80,64},{96,80},{112,96},{128,112},... | collective-permute-start | bytes 786440 | tf_op jit(solution)/shard_map/ppermute | solution.py:45
  78.7 4.2 %collective-permute-done = f32[16,4096]{1,0:T(8,128)S(1)} collective-permute-done((f32[16,4096]{1,0:T(8,128)S(1)}, f32[16,4096]{1,0:T(8,128)S(1)}, u32[]{:S(2)}, u32[]{:S(2)}) %collective-permute-start) | collective-permute-done | bytes 262176 | tf_op jit(solution)/shard_map/ppermute | solution.py:44
  82.9 0.9 collective-permute-done.1
  83.8 0.0 copy-done.4
  83.8 0.0 copy-done.5
  83.8 0.0 copy-start.6
  83.8 4.5 %fusion.315 = (f32[1,16,4096]{2,1,0:T(8,128)S(1)}, f32[1,16,4096]{2,1,0:T(8,128)S(1)}) fusion(f32[16,4096]{1,0:T(8,128)S(1)} %collective-permute-done, f32[3,3,16,4096]{3,2,1,0:T(8,128)} %get-tuple-element.14, f32[3,3,16,4096]{3,2,1,0:T(8,128)S(1)} %copy-done.4, pred[4096]{0:T(1024)(128)(4,1)S(1)} %get-tuple-element.23, pred[4096]{0:T(1024)(128)(4,1)S(1)} %fusion.329, ...), kind=kLoop, calls=%fused_computation.439 | loop fusion | flops 4718592 | bytes 11546624 | tf_op jit(solution)/shard_map/stack | solution.py:59
  88.3 0.0 copy-done.6
  88.3 0.8 fusion.2
  89.2 0.0 all-gather.5.cloned.1.call-update
  89.2 39.9 %all-gather.5.cloned.1.call-done = bf16[2,256,4096]{2,1,0:T(8,128)(2,1)} async-done(((bf16[2,16,4096]{2,1,0:T(8,128)(2,1)}), bf16[2,256,4096]{2,1,0:T(8,128)(2,1)}) %all-gather.5.cloned.1.call-update) | async-done | bytes 4194320 | tf_op jit(solution)/shard_map/all_gather | solution.py:70
  129.1 0.0 copy-done
  129.1 9.2 %fusion.331 = f32[2,4096,432]{1,2,0:T(8,128)} fusion(bf16[432,256,1]{1,0,2:T(8,128)(2,1)S(1)} %bitcast.1056, bf16[2,256,4096]{2,1,0:T(8,128)(2,1)} %all-gather.5.cloned.1.call-done), kind=kOutput, calls=%fused_computation.457 | convolution fusion | flops 1811939328 | bytes 18571264 | tf_op jit(solution)/shard_map/tc,pcq->tpq/dot_general | solution.py:15
  138.3 9.7 %slice_bitcast_fusion.5 = (f32[3,3,16,4096]{3,2,1,0:T(8,128)}, f32[3,3,16,4096]{3,2,1,0:T(8,128)S(1)}, f32[3,3,16,4096]{3,2,1,0:T(8,128)}, f32[3,3,16,4096]{3,2,...) fusion(f32[3,3,3,16,2,4096]{5,3,2,1,0,4:T(8,128)} %bitcast.1057), kind=kLoop, calls=%fused_computation.5 | loop fusion | bytes 28311552 | tf_op jit(solution)/shard_map/squeeze | solution.py:52
  148.0 0.0 copy-start.3
  148.0 2.3 %fusion.211 = f32[16,4096]{1,0:T(8,128)S(1)} fusion(f32[3,3,16,4096]{3,2,1,0:T(8,128)} %get-tuple-element.8, pred[4096]{0:T(1024)(128)(4,1)S(1)} %get-tuple-element.23, pred[4096]{0:T(1024)(128)(4,1)S(1)} %fusion.329, pred[4096]{0:T(1024)(128)(4,1)S(1)} %get-tuple-element.24), kind=kLoop, calls=%fused_computation.323 | loop fusion | flops 1114112 | bytes 2895872 | tf_op jit(solution)/shard_map/add | solution.py:32
  150.4 3.4 %collective-permute-start.2 = (f32[16,4096]{1,0:T(8,128)S(1)}, f32[16,4096]{1,0:T(8,128)S(1)}, u32[]{:S(2)}, u32[]{:S(2)}) collective-permute-start(f32[16,4096]{1,0:T(8,128)S(1)} %fusion.211), channel_id=1, source_target_pairs={{0,16},{16,32},{32,48},{48,64},{64,80},{80,96},{96,112},{112,128},... | collective-permute-start | bytes 786440 | tf_op jit(solution)/shard_map/ppermute | solution.py:44
  153.7 9.8 %collective-permute-done.2 = f32[16,4096]{1,0:T(8,128)S(1)} collective-permute-done((f32[16,4096]{1,0:T(8,128)S(1)}, f32[16,4096]{1,0:T(8,128)S(1)}, u32[]{:S(2)}, u32[]{:S(2)}) %collective-permute-start.2) | collective-permute-done | bytes 262176 | tf_op jit(solution)/shard_map/ppermute | solution.py:44
  163.5 0.0 copy-done.3
  163.5 0.0 copy-start.2
  163.5 4.2 %fusion.313 = (f32[1,16,4096]{2,1,0:T(8,128)S(1)}, f32[16,4096]{1,0:T(8,128)S(1)}) fusion(f32[16,4096]{1,0:T(8,128)S(1)} %collective-permute-done.2, f32[3,3,16,4096]{3,2,1,0:T(8,128)} %get-tuple-element.9, f32[3,3,16,4096]{3,2,1,0:T(8,128)S(1)} %copy-done.3, pred[4096]{0:T(1024)(128)(4,1)S(1)} %get-tuple-element.23, pred[4096]{0:T(1024)(128)(4,1)S(1)} %fusion.329, ...), kind=kLoop, calls=%fused_computation.437 | loop fusion | flops 3473408 | bytes 8663040 | tf_op jit(solution)/shard_map/stack | solution.py:59
  167.7 1.9 %collective-permute-start.3 = (f32[16,4096]{1,0:T(8,128)S(1)}, f32[16,4096]{1,0:T(8,128)S(1)}, u32[]{:S(2)}, u32[]{:S(2)}) collective-permute-start(f32[16,4096]{1,0:T(8,128)S(1)} %get-tuple-element.18), channel_id=1, source_target_pairs={{16,0},{32,16},{48,32},{64,48},{80,64},{96,80},{112,96},{128,112},... | collective-permute-start | bytes 786440 | tf_op jit(solution)/shard_map/ppermute | solution.py:45
  169.6 6.7 %collective-permute-done.3 = f32[16,4096]{1,0:T(8,128)S(1)} collective-permute-done((f32[16,4096]{1,0:T(8,128)S(1)}, f32[16,4096]{1,0:T(8,128)S(1)}, u32[]{:S(2)}, u32[]{:S(2)}) %collective-permute-start.3) | collective-permute-done | bytes 262176 | tf_op jit(solution)/shard_map/ppermute | solution.py:45
  176.3 0.0 copy-start.1
  176.3 0.0 copy-done.2
  176.3 0.0 copy-start.7
  176.3 1.2 fusion.312
  177.5 0.0 copy-done.7
  177.5 0.9 fusion.3
  178.4 0.0 copy-done.1
  (2 shorter events, 0.0 us)
Async XLA Ops:
  6.5 122.6 %copy-start = (bf16[3,3,3,16,256]{4,3,2,1,0:T(8,128)(2,1)S(1)}, bf16[3,3,3,16,256]{4,3,2,1,0:T(8,128)(2,1)}, u32[]{:S(2)}) copy-start(bf16[3,3,3,16,256]{4,3,2,1,0:T(8,128)(2,1)} %param.8) | copy-start | bytes 663556
  6.5 42.0 %all-gather.3.cloned.1.call-start = ((), (), s32[]{:S(2)}) async-start(), calls=%async_computation | async-start | bytes 2228224 | tf_op jit(solution)/shard_map/all_gather | solution.py:68
  7.3 121.8 %all-gather.5.cloned.1.call-start = ((), (), s32[]{:S(2)}) async-start(), calls=%async_computation.1 | async-start | bytes 4456448 | tf_op jit(solution)/shard_map/all_gather | solution.py:70
  66.9 16.9 %copy-start.4 = (f32[3,3,16,4096]{3,2,1,0:T(8,128)S(1)}, f32[3,3,16,4096]{3,2,1,0:T(8,128)}, u32[]{:S(2)}) copy-start(f32[3,3,16,4096]{3,2,1,0:T(8,128)} %get-tuple-element.11) | copy-start | bytes 7077892
  66.9 16.9 %copy-start.5 = (f32[3,3,16,4096]{3,2,1,0:T(8,128)S(1)}, f32[3,3,16,4096]{3,2,1,0:T(8,128)}, u32[]{:S(2)}) copy-start(f32[3,3,16,4096]{3,2,1,0:T(8,128)} %get-tuple-element.12) | copy-start | bytes 7077892
  69.8 13.1 %collective-permute-start = (f32[16,4096]{1,0:T(8,128)S(1)}, f32[16,4096]{1,0:T(8,128)S(1)}, u32[]{:S(2)}, u32[]{:S(2)}) collective-permute-start(f32[16,4096]{1,0:T(8,128)S(1)} %get-tuple-element.21), channel_id=1, source_target_pairs={{0,16},{16,32},{32,48},{48,64},{64,80},{80,96},{96,112},{112,128},... | collective-permute-start | bytes 786440 | tf_op jit(solution)/shard_map/ppermute | solution.py:44
  73.0 10.8 %collective-permute-start.1 = (f32[16,4096]{1,0:T(8,128)S(1)}, f32[16,4096]{1,0:T(8,128)S(1)}, u32[]{:S(2)}, u32[]{:S(2)}) collective-permute-start(f32[16,4096]{1,0:T(8,128)S(1)} %get-tuple-element.22), channel_id=1, source_target_pairs={{16,0},{32,16},{48,32},{64,48},{80,64},{96,80},{112,96},{128,112},... | collective-permute-start | bytes 786440 | tf_op jit(solution)/shard_map/ppermute | solution.py:45
  83.8 4.6 %copy-start.6 = (f32[16]{0:T(128)S(1)}, f32[16]{0:T(128)}, u32[]{:S(2)}) copy-start(f32[16]{0:T(128)} %param.7) | copy-start | bytes 196
  148.0 15.5 %copy-start.3 = (f32[3,3,16,4096]{3,2,1,0:T(8,128)S(1)}, f32[3,3,16,4096]{3,2,1,0:T(8,128)}, u32[]{:S(2)}) copy-start(f32[3,3,16,4096]{3,2,1,0:T(8,128)} %get-tuple-element.5) | copy-start | bytes 7077892
  150.4 13.1 %collective-permute-start.2 = (f32[16,4096]{1,0:T(8,128)S(1)}, f32[16,4096]{1,0:T(8,128)S(1)}, u32[]{:S(2)}, u32[]{:S(2)}) collective-permute-start(f32[16,4096]{1,0:T(8,128)S(1)} %fusion.211), channel_id=1, source_target_pairs={{0,16},{16,32},{32,48},{48,64},{64,80},{80,96},{96,112},{112,128},... | collective-permute-start | bytes 786440 | tf_op jit(solution)/shard_map/ppermute | solution.py:44
  163.5 12.8 %copy-start.2 = (f32[3,3,16,4096]{3,2,1,0:T(8,128)S(1)}, f32[3,3,16,4096]{3,2,1,0:T(8,128)}, u32[]{:S(2)}) copy-start(f32[3,3,16,4096]{3,2,1,0:T(8,128)} %get-tuple-element.7) | copy-start | bytes 7077892
  167.7 8.6 %collective-permute-start.3 = (f32[16,4096]{1,0:T(8,128)S(1)}, f32[16,4096]{1,0:T(8,128)S(1)}, u32[]{:S(2)}, u32[]{:S(2)}) collective-permute-start(f32[16,4096]{1,0:T(8,128)S(1)} %get-tuple-element.18), channel_id=1, source_target_pairs={{16,0},{32,16},{48,32},{64,48},{80,64},{96,80},{112,96},{128,112},... | collective-permute-start | bytes 786440 | tf_op jit(solution)/shard_map/ppermute | solution.py:45
  176.3 2.1 %copy-start.1 = (bf16[3,3,3,16,256]{4,3,2,1,0:T(8,128)(2,1)S(1)}, bf16[3,3,3,16,256]{4,3,2,1,0:T(8,128)(2,1)}, u32[]{:S(2)}) copy-start(bf16[3,3,3,16,256]{4,3,2,1,0:T(8,128)(2,1)} %param.8) | copy-start | bytes 663556
  176.3 1.3 copy-start.7
Sparse Core Ops, SparseCore 0:
  9.2 39.2 all-gather.2
  89.3 39.7 all-gather.4
where the time goes:
time: 187 us; the launch traced here: 185 us
  waiting for transfers between devices  103 us (55%)
  local copies, waits for them, and re-layouts  19.4 us (10%)
  matrix products  17.9 us (10%)
  other arithmetic  16.9 us (9%)
  starting transfers between devices  14.2 us (8%)
  between operations  13.5 us (7%)
    all_gather x1, waiting for transfers between devices, local(): whole_in = lax.all_gather(features, 'filt', axis=1, tiled=True)  41.2 us
    all_gather x1, waiting for transfers between devices, local(): whole_mid = lax.all_gather(hidden, 'filt', axis=1, tiled=True)  39.9 us
    squeeze x2, local copies, waits for them, and re-layouts, conv_sum(): piece = spatial_sum(products[tap_d, :, :, :, source])  19.4 us
    dot_general x2, matrix products, tap_products(): jnp.einsum('tc,pcq->tpq', taps, block, preferred_element_type=jnp.float32)  17.9 us
    ppermute x2, waiting for transfers between devices, conv_sum(): from_below = lax.ppermute(to_above, 'depth', forward)  14 us
    another operation x3, other arithmetic, conv_sum(): return jnp.stack(rows)  9.94 us
    ppermute x2, starting transfers between devices, conv_sum(): from_above = lax.ppermute(to_below, 'depth', backward)  7.64 us
    ppermute x2, waiting for transfers between devices, conv_sum(): from_above = lax.ppermute(to_below, 'depth', backward)  7.53 us
  transfers between devices with their start and end apart: 6, of which 6 were waited for; matrix products, arithmetic and copies ran while one was open for 0% of the time, Pallas kernels for 0%

commit v1 on v0

--- a/solution.py
+++ b/solution.py
@@ -9,11 +9,11 @@
 leak_slope = 0.3
 
 
-def tap_products(block, kernel):
-    outs, chans = kernel.shape[3], kernel.shape[4]
-    taps = kernel.reshape(27 * outs, chans)
-    products = jnp.einsum("tc,pcq->tpq", taps, block, preferred_element_type=jnp.float32)
-    return products.reshape(3, 3, 3, outs, block.shape[0], block.shape[2])
+def tap_products(plane, kernel_d):
+    outs, chans = kernel_d.shape[2], kernel_d.shape[3]
+    taps = kernel_d.reshape(9 * outs, chans)
+    products = jnp.einsum("tc,cq->tq", taps, plane, preferred_element_type=jnp.float32)
+    return products.reshape(3, 3, outs, plane.shape[1])
 
 
 def spatial_sum(part):
@@ -35,12 +35,15 @@
 
 def conv_sum(block, kernel):
     planes = block.shape[0]
-    products = tap_products(block, kernel)
+
+    def part(tap_d, source):
+        return spatial_sum(tap_products(block[source], kernel[tap_d]))
+
     count = lax.axis_size("depth")
     forward = [(i, i + 1) for i in range(count - 1)]
     backward = [(i + 1, i) for i in range(count - 1)]
-    to_above = spatial_sum(products[0, :, :, :, planes - 1])
-    to_below = spatial_sum(products[2, :, :, :, 0])
+    to_above = part(0, planes - 1)
+    to_below = part(2, 0)
     from_below = lax.ppermute(to_above, "depth", forward)
     from_above = lax.ppermute(to_below, "depth", backward)
     rows = []
@@ -49,7 +52,7 @@
         for tap_d in range(3):
             source = plane + tap_d - 1
             if 0 <= source < planes:
-                piece = spatial_sum(products[tap_d, :, :, :, source])
+                piece = part(tap_d, source)
                 total = piece if total is None else total + piece
         if plane == 0:
             total = total + from_below

time: 187 us -> 146 us (0.78)
  local copies, waits for them, and re-layouts: 19.4 us -> 0.1 us
  matrix products: 17.9 us -> 8.76 us
  other arithmetic: 16.9 us -> 8.74 us
  waiting for transfers between devices: 103 us -> 99.1 us
    squeeze x2 -> x0, local copies, waits for them, and re-layouts: 19.4 us -> none  [conv_sum(): piece = spatial_sum(products[tap_d, :, :, :, source])]
    dot_general x2 -> x12, matrix products: 17.9 us -> 8.76 us  [tap_products(): jnp.einsum('tc,cq->tq', taps, plane, preferred_element_type=jnp.float32)]
    another operation x3, other arithmetic: 9.94 us -> 5.17 us  [conv_sum(): return jnp.stack(rows)]
    ppermute x2, waiting for transfers between devices: 14 us -> 10.3 us  [conv_sum(): from_below = lax.ppermute(to_above, 'depth', forward)]
    add x2, other arithmetic: 5.22 us -> 1.85 us  [spatial_sum(): total = window if total is None else total + window]
  transfers between devices with their start and end apart: 6 -> 6, of which waited for: 6 -> 6; matrix products, arithmetic and copies ran while one was open for 0% -> 3% of each run, Pallas kernels for 0% -> 0%
where the time goes in v1:
time: 146 us; the launch traced here: 144 us
  waiting for transfers between devices  99.1 us (68%)
  starting transfers between devices  14 us (10%)
  between operations  13.6 us (9%)
  matrix products  8.76 us (6%)
  other arithmetic  8.74 us (6%)
    all_gather x1, waiting for transfers between devices, local(): whole_in = lax.all_gather(features, 'filt', axis=1, tiled=True)  41.2 us
    all_gather x1, waiting for transfers between devices, local(): whole_mid = lax.all_gather(hidden, 'filt', axis=1, tiled=True)  39.8 us
    ppermute x2, waiting for transfers between devices, conv_sum(): from_below = lax.ppermute(to_above, 'depth', forward)  10.3 us
    dot_general x12, matrix products, tap_products(): jnp.einsum('tc,cq->tq', taps, plane, preferred_element_type=jnp.float32)  8.76 us
    ppermute x2, starting transfers between devices, conv_sum(): from_above = lax.ppermute(to_below, 'depth', backward)  7.63 us
    ppermute x2, waiting for transfers between devices, conv_sum(): from_above = lax.ppermute(to_below, 'depth', backward)  7.05 us
    ppermute x2, starting transfers between devices, conv_sum(): from_below = lax.ppermute(to_above, 'depth', forward)  6.36 us
    another operation x3, other arithmetic, conv_sum(): return jnp.stack(rows)  5.17 us
  transfers between devices with their start and end apart: 6, of which 6 were waited for; matrix products, arithmetic and copies ran while one was open for 3% of the time, Pallas kernels for 0%

profile of v1, /device:TPU:17, one launch (start us, length us, event | category | flops | bytes accessed | tf_op | source)
XLA Modules:
  0.0 144.3 jit_solution(16713100208393763334)
XLA Ops:
  6.5 0.0 copy-start.2
  6.5 0.0 all-gather.3.cloned.1.call-start
  6.5 0.7 all-gather.3.cloned.1.call-update
  7.3 0.0 all-gather.5.cloned.1.call-start
  7.3 41.2 %all-gather.3.cloned.1.call-done = bf16[2,128,4096]{2,1,0:T(8,128)(2,1)} async-done(((bf16[2,8,4096]{2,1,0:T(8,128)(2,1)}), bf16[2,128,4096]{2,1,0:T(8,128)(2,1)}) %all-gather.3.cloned.1.call-update) | async-done | bytes 2097168 | tf_op jit(solution)/shard_map/all_gather | solution.py:71
  48.5 0.0 copy-start.1
  48.5 1.8 %fusion.10 = f32[3,3,16,4096]{3,2,1,0:T(8,128)S(1)} fusion(bf16[2,128,4096]{2,1,0:T(8,128)(2,1)} %all-gather.3.cloned.1.call-done, bf16[3,3,3,16,128]{4,3,2,1,0:T(8,128)(2,1)} %param.6), kind=kOutput, calls=%fused_computation.112 | convolution fusion | flops 150994944 | bytes 3444736 | tf_op jit(solution)/shard_map/tc,cq->tq/dot_general | solution.py:15
  50.3 0.0 copy-done.2
  50.4 0.1 copy-done.1
  50.4 0.5 fusion.6
  50.9 1.2 fusion.73
  52.1 3.2 %collective-permute-start = (f32[16,4096]{1,0:T(8,128)S(1)}, f32[16,4096]{1,0:T(8,128)S(1)}, u32[]{:S(2)}, u32[]{:S(2)}) collective-permute-start(f32[16,4096]{1,0:T(8,128)S(1)} %get-tuple-element.12), channel_id=1, source_target_pairs={{0,16},{16,32},{32,48},{48,64},{64,80},{80,96},{96,112},{112,128},... | collective-permute-start | bytes 786440 | tf_op jit(solution)/shard_map/ppermute | solution.py:47
  55.3 5.7 %collective-permute-start.1 = (f32[16,4096]{1,0:T(8,128)S(1)}, f32[16,4096]{1,0:T(8,128)S(1)}, u32[]{:S(2)}, u32[]{:S(2)}) collective-permute-start(f32[16,4096]{1,0:T(8,128)S(1)} %get-tuple-element.13), channel_id=1, source_target_pairs={{16,0},{32,16},{48,32},{64,48},{80,64},{96,80},{112,96},{128,112},... | collective-permute-start | bytes 786440 | tf_op jit(solution)/shard_map/ppermute | solution.py:48
  61.0 0.5 fusion.11
  61.5 0.5 fusion.7
  62.0 0.5 fusion.8
  62.4 0.5 fusion.9
  62.9 0.0 copy-start.4
  62.9 0.0 copy-start.3
  62.9 2.4 %collective-permute-done = f32[16,4096]{1,0:T(8,128)S(1)} collective-permute-done((f32[16,4096]{1,0:T(8,128)S(1)}, f32[16,4096]{1,0:T(8,128)S(1)}, u32[]{:S(2)}, u32[]{:S(2)}) %collective-permute-start) | collective-permute-done | bytes 262176 | tf_op jit(solution)/shard_map/ppermute | solution.py:47
  65.3 0.9 collective-permute-done.1
  66.1 2.2 %fusion.325 = (f32[1,16,4096]{2,1,0:T(8,128)S(1)}, f32[1,16,4096]{2,1,0:T(8,128)S(1)}) fusion(f32[16,4096]{1,0:T(8,128)S(1)} %collective-permute-done, f32[3,3,16,4096]{3,2,1,0:T(8,128)S(1)} %fusion.11, f32[3,3,16,4096]{3,2,1,0:T(8,128)S(1)} %fusion.8, pred[4096]{0:T(1024)(128)(4,1)S(1)} %get-tuple-element.14, pred[4096]{0:T(1024)(128)(4,1)S(1)} %fusion.350, ...), kind=kLoop, calls=%fused_computation.441 | loop fusion | flops 4718592 | bytes 11546624 | tf_op jit(solution)/shard_map/stack | solution.py:62
  68.4 0.0 copy-done.4
  68.4 0.8 fusion.12
  69.2 0.0 all-gather.5.cloned.1.call-update
  69.3 0.0 copy-done.3
  69.3 39.8 %all-gather.5.cloned.1.call-done = bf16[2,256,4096]{2,1,0:T(8,128)(2,1)} async-done(((bf16[2,16,4096]{2,1,0:T(8,128)(2,1)}), bf16[2,256,4096]{2,1,0:T(8,128)(2,1)}) %all-gather.5.cloned.1.call-update) | async-done | bytes 4194320 | tf_op jit(solution)/shard_map/all_gather | solution.py:73
  109.1 0.0 copy-start
  109.1 2.2 %fusion.4 = f32[4096,144]{0,1:T(8,128)S(1)} fusion(bf16[144,256]{1,0:T(8,128)(2,1)S(1)} %bitcast.1070, bf16[2,256,4096]{2,1,0:T(8,128)(2,1)} %all-gather.5.cloned.1.call-done), kind=kOutput, calls=%fused_computation.102 | convolution fusion | flops 301989888 | bytes 4530176 | tf_op jit(solution)/shard_map/tc,cq->tq/dot_general | solution.py:15
  111.4 0.6 fusion.221
  112.0 3.2 %collective-permute-start.2 = (f32[16,4096]{1,0:T(8,128)S(1)}, f32[16,4096]{1,0:T(8,128)S(1)}, u32[]{:S(2)}, u32[]{:S(2)}) collective-permute-start(f32[16,4096]{1,0:T(8,128)S(1)} %fusion.221), channel_id=1, source_target_pairs={{0,16},{16,32},{32,48},{48,64},{64,80},{80,96},{96,112},{112,128},... | collective-permute-start | bytes 786440 | tf_op jit(solution)/shard_map/ppermute | solution.py:47
  115.2 0.0 copy-done
  115.2 0.5 fusion.2
  115.7 0.5 fusion.3
  116.2 0.5 fusion.1
  116.6 0.5 fusion
  117.1 8.0 %collective-permute-done.2 = f32[16,4096]{1,0:T(8,128)S(1)} collective-permute-done((f32[16,4096]{1,0:T(8,128)S(1)}, f32[16,4096]{1,0:T(8,128)S(1)}, u32[]{:S(2)}, u32[]{:S(2)}) %collective-permute-start.2) | collective-permute-done | bytes 262176 | tf_op jit(solution)/shard_map/ppermute | solution.py:47
  125.1 1.7 %fusion.323 = (f32[1,16,4096]{2,1,0:T(8,128)S(1)}, f32[16,4096]{1,0:T(8,128)S(1)}) fusion(f32[16,4096]{1,0:T(8,128)S(1)} %collective-permute-done.2, f32[3,3,16,4096]{3,2,1,0:T(8,128)S(1)} %bitcast.1064, f32[3,3,16,4096]{3,2,1,0:T(8,128)S(1)} %bitcast.1066, pred[4096]{0:T(1024)(128)(4,1)S(1)} %get-tuple-element.14, pred[4096]{0:T(1024)(128)(4,1)S(1)} %fusion.350, ...), kind=kLoop, calls=%fused_computation.439 | loop fusion | flops 3473408 | bytes 8663040 | tf_op jit(solution)/shard_map/stack | solution.py:62
  126.8 1.9 %collective-permute-start.3 = (f32[16,4096]{1,0:T(8,128)S(1)}, f32[16,4096]{1,0:T(8,128)S(1)}, u32[]{:S(2)}, u32[]{:S(2)}) collective-permute-start(f32[16,4096]{1,0:T(8,128)S(1)} %get-tuple-element.9), channel_id=1, source_target_pairs={{16,0},{32,16},{48,32},{64,48},{80,64},{96,80},{112,96},{128,112},... | collective-permute-start | bytes 786440 | tf_op jit(solution)/shard_map/ppermute | solution.py:48
  128.7 0.5 fusion.5
  129.2 6.2 %collective-permute-done.3 = f32[16,4096]{1,0:T(8,128)S(1)} collective-permute-done((f32[16,4096]{1,0:T(8,128)S(1)}, f32[16,4096]{1,0:T(8,128)S(1)}, u32[]{:S(2)}, u32[]{:S(2)}) %collective-permute-start.3) | collective-permute-done | bytes 262176 | tf_op jit(solution)/shard_map/ppermute | solution.py:48
  135.4 0.0 copy-start.5
  135.4 1.2 fusion.322
  136.6 0.0 copy-done.5
  136.7 0.8 fusion.13
  (3 shorter events, 0.0 us)
Async XLA Ops:
  6.5 43.8 %copy-start.2 = (bf16[3,3,3,16,128]{4,3,2,1,0:T(8,128)(2,1)S(1)}, bf16[3,3,3,16,128]{4,3,2,1,0:T(8,128)(2,1)}, u32[]{:S(2)}) copy-start(bf16[3,3,3,16,128]{4,3,2,1,0:T(8,128)(2,1)} %param.6) | copy-start | bytes 331780
  6.5 42.0 %all-gather.3.cloned.1.call-start = ((), (), s32[]{:S(2)}) async-start(), calls=%async_computation | async-start | bytes 2228224 | tf_op jit(solution)/shard_map/all_gather | solution.py:71
  7.3 101.9 %all-gather.5.cloned.1.call-start = ((), (), s32[]{:S(2)}) async-start(), calls=%async_computation.1 | async-start | bytes 4456448 | tf_op jit(solution)/shard_map/all_gather | solution.py:73
  48.5 1.9 %copy-start.1 = (bf16[2,128,4096]{2,1,0:T(8,128)(2,1)S(1)}, bf16[2,128,4096]{2,1,0:T(8,128)(2,1)}, u32[]{:S(2)}) copy-start(bf16[2,128,4096]{2,1,0:T(8,128)(2,1)} %all-gather.3.cloned.1.call-done) | copy-start | bytes 6291460
  52.1 13.1 %collective-permute-start = (f32[16,4096]{1,0:T(8,128)S(1)}, f32[16,4096]{1,0:T(8,128)S(1)}, u32[]{:S(2)}, u32[]{:S(2)}) collective-permute-start(f32[16,4096]{1,0:T(8,128)S(1)} %get-tuple-element.12), channel_id=1, source_target_pairs={{0,16},{16,32},{32,48},{48,64},{64,80},{80,96},{96,112},{112,128},... | collective-permute-start | bytes 786440 | tf_op jit(solution)/shard_map/ppermute | solution.py:47
  55.3 10.8 %collective-permute-start.1 = (f32[16,4096]{1,0:T(8,128)S(1)}, f32[16,4096]{1,0:T(8,128)S(1)}, u32[]{:S(2)}, u32[]{:S(2)}) collective-permute-start(f32[16,4096]{1,0:T(8,128)S(1)} %get-tuple-element.13), channel_id=1, source_target_pairs={{16,0},{32,16},{48,32},{64,48},{80,64},{96,80},{112,96},{128,112},... | collective-permute-start | bytes 786440 | tf_op jit(solution)/shard_map/ppermute | solution.py:48
  62.9 5.5 %copy-start.4 = (f32[16]{0:T(128)S(1)}, f32[16]{0:T(128)}, u32[]{:S(2)}) copy-start(f32[16]{0:T(128)} %param.7) | copy-start | bytes 196
  62.9 6.4 %copy-start.3 = (bf16[3,3,3,16,256]{4,3,2,1,0:T(8,128)(2,1)S(1)}, bf16[3,3,3,16,256]{4,3,2,1,0:T(8,128)(2,1)}, u32[]{:S(2)}) copy-start(bf16[3,3,3,16,256]{4,3,2,1,0:T(8,128)(2,1)} %param.8) | copy-start | bytes 663556
  109.1 6.0 %copy-start = (bf16[2,256,4096]{2,1,0:T(8,128)(2,1)S(1)}, bf16[2,256,4096]{2,1,0:T(8,128)(2,1)}, u32[]{:S(2)}) copy-start(bf16[2,256,4096]{2,1,0:T(8,128)(2,1)} %all-gather.5.cloned.1.call-done) | copy-start | bytes 12582916
  112.0 13.1 %collective-permute-start.2 = (f32[16,4096]{1,0:T(8,128)S(1)}, f32[16,4096]{1,0:T(8,128)S(1)}, u32[]{:S(2)}, u32[]{:S(2)}) collective-permute-start(f32[16,4096]{1,0:T(8,128)S(1)} %fusion.221), channel_id=1, source_target_pairs={{0,16},{16,32},{32,48},{48,64},{64,80},{80,96},{96,112},{112,128},... | collective-permute-start | bytes 786440 | tf_op jit(solution)/shard_map/ppermute | solution.py:47
  126.8 8.6 %collective-permute-start.3 = (f32[16,4096]{1,0:T(8,128)S(1)}, f32[16,4096]{1,0:T(8,128)S(1)}, u32[]{:S(2)}, u32[]{:S(2)}) collective-permute-start(f32[16,4096]{1,0:T(8,128)S(1)} %get-tuple-element.9), channel_id=1, source_target_pairs={{16,0},{32,16},{48,32},{64,48},{80,64},{96,80},{112,96},{128,112},... | collective-permute-start | bytes 786440 | tf_op jit(solution)/shard_map/ppermute | solution.py:48
  135.4 1.2 copy-start.5
Sparse Core Ops, SparseCore 0:
  9.2 39.2 all-gather.2
  69.4 39.7 all-gather.4
